TPU v7x, 256 devices: a whole 4x4x8 slice. The times are simulated.
256 devices in a mesh: sample: 8 (over z_lo, y), space: 32 (over x, z_hi, core).
Axes of the slice: x: 4, y: 4, z: 8 (z_hi: 4, z_lo: 2; z = z_hi * 2 + z_lo), core: 2. Of those that a mesh axis runs over, the one named last changes fastest.
Arguments:
- volume: bfloat16 [64, 8, 32, 1024], P('space', 'sample'), may hold values from -6 to 6
- out_grads: bfloat16 [32, 8, 128, 256], P('space', 'sample'), may hold values from -6 to 6
- kernel_one: bfloat16 [27, 32, 64], replicated, may hold values from -0.21875 to 0.21875
- kernel_two: bfloat16 [27, 64, 128], replicated, may hold values from -0.15625 to 0.15625
Outputs:
- layer_out: bfloat16 [32, 8, 128, 256], P('space', 'sample')
- input_grads: bfloat16 [64, 8, 32, 1024], P('space', 'sample')
- kernel_one_grads: float32 [27, 32, 64], replicated
- kernel_two_grads: float32 [27, 64, 128], replicated
All inputs are finite; a program needn't handle non-finite values.
Results may differ from a plain program's by a relative error of at most 0.015.
Values may be sent and summed in bfloat16 or wider, within the bound.
No kernel may reach another device: no remote copies, remote signals or barrier semaphores. Data moves between devices by JAX's collectives and lax.ppermute only.
A program may use at most 128 MiB of HBM per device.

v0:
```python
import jax
import jax.numpy as jnp
from jax import lax
from jax.sharding import PartitionSpec as P

SIDE = 32


def with_halo(block, sides, width):
    for axis, dim in sides:
        count = lax.axis_size(axis)
        forward = [(i, i + 1) for i in range(count - 1)]
        backward = [(target, source) for source, target in forward]
        low = lax.ppermute(
            lax.slice_in_dim(block, block.shape[dim] - width, None, axis=dim), axis, forward
        )
        high = lax.ppermute(lax.slice_in_dim(block, 0, width, axis=dim), axis, backward)
        block = jnp.concatenate([low, block, high], axis=dim)
    return block


def passed_along(block, axis, distance):
    devices = range(lax.axis_size(axis))
    route = [(i - distance, i) for i in devices if i - distance in devices]
    return lax.ppermute(block, axis, route)


def convolve(inputs, kernel, stride, margins, dilation):
    return lax.conv_general_dilated(
        inputs,
        kernel,
        (stride, stride, stride),
        margins,
        lhs_dilation=(dilation, dilation, dilation),
        dimension_numbers=("DNCHW", "DHWIO", "DNCHW"),
        preferred_element_type=jnp.float32,
    )


def kernel_cube(kernel):
    return kernel.reshape(3, 3, 3, kernel.shape[1], kernel.shape[2])


def reversed_kernel(kernel):
    cube = kernel_cube(kernel)
    return jnp.transpose(cube[::-1, ::-1, ::-1], (0, 1, 2, 4, 3))


def weight_grad(padded, grads, stride):
    depth_out, rows_out, cols_out = (grads.shape[0], grads.shape[3], grads.shape[4])
    terms = []
    for depth_tap in range(3):
        for row_tap in range(3):
            for col_tap in range(3):
                window = lax.slice(
                    padded,
                    (depth_tap, 0, 0, row_tap, col_tap),
                    (
                        depth_tap + stride * (depth_out - 1) + 1,
                        padded.shape[1],
                        padded.shape[2],
                        row_tap + stride * (rows_out - 1) + 1,
                        col_tap + stride * (cols_out - 1) + 1,
                    ),
                    (stride, 1, 1, stride, stride),
                )
                terms.append(
                    jnp.einsum("zbiyx,zboyx->io", window, grads, preferred_element_type=jnp.float32)
                )
    return jnp.stack(terms)


def local(volume, out_grads, kernel_one, kernel_two):
    depth, batch, channels_in, plane = volume.shape
    channels_two = kernel_two.shape[2]
    half_side = SIDE // 2
    space_count = lax.axis_size("space")
    sample_count = lax.axis_size("sample")
    scale_one = float(sample_count * batch * space_count * depth * plane) ** (-0.5)
    scale_two = scale_one * 8.0**0.5
    cells = volume.reshape(depth, batch, channels_in, SIDE, SIDE)
    grads_cells = out_grads.reshape(depth // 2, batch, channels_two, half_side, half_side)
    framed = with_halo(cells, (("space", 0),), 1)
    pre_one = convolve(framed, kernel_cube(kernel_one), 1, [(0, 0), (1, 1), (1, 1)], 1)
    hidden = jax.nn.silu(pre_one).astype(jnp.bfloat16)
    below = passed_along(hidden[-1:], "space", 1)
    stacked = jnp.pad(jnp.concatenate([below, hidden], 0), ((0, 0), (0, 0), (0, 0), (1, 1), (1, 1)))
    strided = convolve(stacked, kernel_cube(kernel_two), 2, [(0, 0), (0, 0), (0, 0)], 1)
    above = passed_along(grads_cells, "space", -1)
    spread = convolve(
        jnp.concatenate([grads_cells, above], 0),
        reversed_kernel(kernel_two),
        1,
        [(1, 0), (1, 2), (1, 2)],
        2,
    )
    hidden_grads = spread.astype(jnp.bfloat16)
    local_two = weight_grad(stacked, grads_cells, 2) * scale_two
    second_grads = lax.psum(local_two, ("sample", "space"))
    layer_out = strided.astype(jnp.bfloat16).reshape(depth // 2, batch, channels_two, plane // 4)
    sigma = jax.nn.sigmoid(pre_one)
    pre_grads = (hidden_grads.astype(jnp.float32) * sigma * (1.0 + pre_one * (1.0 - sigma))).astype(
        jnp.bfloat16
    )
    framed_grads = with_halo(pre_grads, (("space", 0),), 1)
    input_grads = convolve(
        framed_grads, reversed_kernel(kernel_one), 1, [(0, 0), (1, 1), (1, 1)], 1
    ).astype(jnp.bfloat16)
    padded_input = jnp.pad(framed, ((0, 0), (0, 0), (0, 0), (1, 1), (1, 1)))
    first_grads = weight_grad(padded_input, pre_grads, 1) * scale_one
    first_grads = lax.psum(first_grads, ("sample", "space"))
    return (
        layer_out,
        input_grads.reshape(depth, batch, channels_in, plane),
        first_grads,
        second_grads,
    )


def solution(mesh):
    in_specs = (P("space", "sample", None, None), P("space", "sample", None, None), P(), P())
    out_specs = (P("space", "sample", None, None), P("space", "sample", None, None), P(), P())
    return jax.shard_map(local, mesh=mesh, in_specs=in_specs, out_specs=out_specs, check_vma=False)
```

profile of v0, /device:TPU:1, one launch (start us, length us, event | category | flops | bytes accessed | tf_op | source)
XLA Modules:
  0.0 470.1 jit_solution(3152484372003187827)
XLA Ops:
  7.2 0.9 fusion.282
  8.8 5.1 %collective-permute-start.1 = (bf16[1,1,32,32,32]{3,2,0,4,1:T(8,128)(2,1)S(1)}, bf16[1,1,32,32,32]{3,2,0,4,1:T(8,128)(2,1)S(1)}, u32[]{:S(2)}, u32[]{:S(2)}) collective-permute-start(bf16[1,1,32,32,32]{3,2,0,4,1:T(8,128)(2,1)S(1)} %copy.119), channel_id=1, source_target_pairs={{1,0},{2,1},{3,2},{4,3},{5,4},{6,5},{7,6},{8,7},{9,8},{10,9},{11,1... | collective-permute-start | bytes 196616 | tf_op jit(solution)/shard_map/ppermute | solution.py:17
  14.6 3.1 collective-permute-start
  17.8 1.9 collective-permute-start.3
  20.5 0.9 copy.120
  21.4 1.6 copy.157
  24.1 1.6 copy.123
  25.7 1.2 slice.285
  27.0 3.8 add_divide_fusion
  31.0 4.5 collective-permute-start.2
  36.8 0.8 fusion.24
  38.5 1.9 collective-permute-start.5
  40.5 4.7 %collective-permute-start.4 = (bf16[1,1,64,32,32]{2,3,4,0,1:T(8,128)(2,1)S(1)}, bf16[1,1,64,32,32]{2,3,4,0,1:T(8,128)(2,1)}, u32[]{:S(2)}, u32[]{:S(2)}) collective-permute-start(bf16[1,1,64,32,32]{2,3,4,0,1:T(8,128)(2,1)S(1)} %get-tuple-element.21), channel_id=1, source_target_pairs={{0,1},{1,2},{2,3},{3,4},{4,5},{5,6},{6,7},{7,8},{8,9},{9,10},{10,1... | collective-permute-start | bytes 393224 | tf_op jit(solution)/shard_map/ppermute | solution.py:14
  45.7 0.6 fusion.92
  46.3 0.6 fusion.91
  48.3 0.6 fusion.87
  48.8 0.6 fusion.86
  49.4 0.6 fusion.85
  50.0 0.6 fusion.84
  50.5 0.6 fusion.83
  51.1 0.6 fusion.82
  52.9 0.6 fusion.79
  54.0 0.6 fusion.77
  54.6 0.6 fusion.76
  55.7 0.6 fusion.74
  57.6 0.6 fusion.70
  58.7 0.6 fusion.68
  59.3 0.8 broadcast_multiply_fusion.1
  60.6 5.1 %slice.246 = bf16[1,1,64,16,16]{2,3,4,1,0:T(8,128)(2,1)} slice(bf16[3,1,64,34,34]{2,3,4,1,0:T(8,128)(2,1)S(1)} %pad.9), slice={[0:1:1], [0:1:1], [0:64:1], [0:31:2], [0:31:2]} | slice | bytes 65536 | tf_op jit(solution)/shard_map/slice | solution.py:55
  65.7 4.9 %slice.247 = bf16[1,1,64,16,16]{2,3,4,1,0:T(8,128)(2,1)} slice(bf16[3,1,64,34,34]{2,3,4,1,0:T(8,128)(2,1)S(1)} %pad.9), slice={[0:1:1], [0:1:1], [0:64:1], [0:31:2], [1:32:2]} | slice | bytes 65536 | tf_op jit(solution)/shard_map/slice | solution.py:55
  70.6 4.9 %slice.248 = bf16[1,1,64,16,16]{2,3,4,1,0:T(8,128)(2,1)} slice(bf16[3,1,64,34,34]{2,3,4,1,0:T(8,128)(2,1)S(1)} %pad.9), slice={[0:1:1], [0:1:1], [0:64:1], [0:31:2], [2:33:2]} | slice | bytes 65536 | tf_op jit(solution)/shard_map/slice | solution.py:55
  75.5 4.9 %slice.249 = bf16[1,1,64,16,16]{2,3,4,1,0:T(8,128)(2,1)} slice(bf16[3,1,64,34,34]{2,3,4,1,0:T(8,128)(2,1)S(1)} %pad.9), slice={[0:1:1], [0:1:1], [0:64:1], [1:32:2], [0:31:2]} | slice | bytes 65536 | tf_op jit(solution)/shard_map/slice | solution.py:55
  80.4 4.9 %slice.250 = bf16[1,1,64,16,16]{2,3,4,1,0:T(8,128)(2,1)} slice(bf16[3,1,64,34,34]{2,3,4,1,0:T(8,128)(2,1)S(1)} %pad.9), slice={[0:1:1], [0:1:1], [0:64:1], [1:32:2], [1:32:2]} | slice | bytes 65536 | tf_op jit(solution)/shard_map/slice | solution.py:55
  85.2 4.9 %slice.251 = bf16[1,1,64,16,16]{2,3,4,1,0:T(8,128)(2,1)} slice(bf16[3,1,64,34,34]{2,3,4,1,0:T(8,128)(2,1)S(1)} %pad.9), slice={[0:1:1], [0:1:1], [0:64:1], [1:32:2], [2:33:2]} | slice | bytes 65536 | tf_op jit(solution)/shard_map/slice | solution.py:55
  90.1 4.9 %slice.252 = bf16[1,1,64,16,16]{2,3,4,1,0:T(8,128)(2,1)} slice(bf16[3,1,64,34,34]{2,3,4,1,0:T(8,128)(2,1)S(1)} %pad.9), slice={[0:1:1], [0:1:1], [0:64:1], [2:33:2], [0:31:2]} | slice | bytes 65536 | tf_op jit(solution)/shard_map/slice | solution.py:55
  95.0 4.9 %slice.253 = bf16[1,1,64,16,16]{2,3,4,1,0:T(8,128)(2,1)} slice(bf16[3,1,64,34,34]{2,3,4,1,0:T(8,128)(2,1)S(1)} %pad.9), slice={[0:1:1], [0:1:1], [0:64:1], [2:33:2], [1:32:2]} | slice | bytes 65536 | tf_op jit(solution)/shard_map/slice | solution.py:55
  99.9 4.9 %slice.254 = bf16[1,1,64,16,16]{2,3,4,1,0:T(8,128)(2,1)} slice(bf16[3,1,64,34,34]{2,3,4,1,0:T(8,128)(2,1)S(1)} %pad.9), slice={[0:1:1], [0:1:1], [0:64:1], [2:33:2], [2:33:2]} | slice | bytes 65536 | tf_op jit(solution)/shard_map/slice | solution.py:55
  104.8 4.9 %slice.255 = bf16[1,1,64,16,16]{2,3,4,1,0:T(8,128)(2,1)} slice(bf16[3,1,64,34,34]{2,3,4,1,0:T(8,128)(2,1)S(1)} %pad.9), slice={[1:2:1], [0:1:1], [0:64:1], [0:31:2], [0:31:2]} | slice | bytes 65536 | tf_op jit(solution)/shard_map/slice | solution.py:55
  109.6 4.9 %slice.256 = bf16[1,1,64,16,16]{2,3,4,1,0:T(8,128)(2,1)} slice(bf16[3,1,64,34,34]{2,3,4,1,0:T(8,128)(2,1)S(1)} %pad.9), slice={[1:2:1], [0:1:1], [0:64:1], [0:31:2], [1:32:2]} | slice | bytes 65536 | tf_op jit(solution)/shard_map/slice | solution.py:55
  114.5 4.9 %slice.257 = bf16[1,1,64,16,16]{2,3,4,1,0:T(8,128)(2,1)} slice(bf16[3,1,64,34,34]{2,3,4,1,0:T(8,128)(2,1)S(1)} %pad.9), slice={[1:2:1], [0:1:1], [0:64:1], [0:31:2], [2:33:2]} | slice | bytes 65536 | tf_op jit(solution)/shard_map/slice | solution.py:55
  119.4 4.9 %slice.258 = bf16[1,1,64,16,16]{2,3,4,1,0:T(8,128)(2,1)} slice(bf16[3,1,64,34,34]{2,3,4,1,0:T(8,128)(2,1)S(1)} %pad.9), slice={[1:2:1], [0:1:1], [0:64:1], [1:32:2], [0:31:2]} | slice | bytes 65536 | tf_op jit(solution)/shard_map/slice | solution.py:55
  124.3 4.9 %slice.259 = bf16[1,1,64,16,16]{2,3,4,1,0:T(8,128)(2,1)} slice(bf16[3,1,64,34,34]{2,3,4,1,0:T(8,128)(2,1)S(1)} %pad.9), slice={[1:2:1], [0:1:1], [0:64:1], [1:32:2], [1:32:2]} | slice | bytes 65536 | tf_op jit(solution)/shard_map/slice | solution.py:55
  129.2 4.9 %slice.260 = bf16[1,1,64,16,16]{2,3,4,1,0:T(8,128)(2,1)} slice(bf16[3,1,64,34,34]{2,3,4,1,0:T(8,128)(2,1)S(1)} %pad.9), slice={[1:2:1], [0:1:1], [0:64:1], [1:32:2], [2:33:2]} | slice | bytes 65536 | tf_op jit(solution)/shard_map/slice | solution.py:55
  134.0 4.9 %slice.261 = bf16[1,1,64,16,16]{2,3,4,1,0:T(8,128)(2,1)} slice(bf16[3,1,64,34,34]{2,3,4,1,0:T(8,128)(2,1)S(1)} %pad.9), slice={[1:2:1], [0:1:1], [0:64:1], [2:33:2], [0:31:2]} | slice | bytes 65536 | tf_op jit(solution)/shard_map/slice | solution.py:55
  138.9 4.9 %slice.262 = bf16[1,1,64,16,16]{2,3,4,1,0:T(8,128)(2,1)} slice(bf16[3,1,64,34,34]{2,3,4,1,0:T(8,128)(2,1)S(1)} %pad.9), slice={[1:2:1], [0:1:1], [0:64:1], [2:33:2], [1:32:2]} | slice | bytes 65536 | tf_op jit(solution)/shard_map/slice | solution.py:55
  143.8 4.9 %slice.263 = bf16[1,1,64,16,16]{2,3,4,1,0:T(8,128)(2,1)} slice(bf16[3,1,64,34,34]{2,3,4,1,0:T(8,128)(2,1)S(1)} %pad.9), slice={[1:2:1], [0:1:1], [0:64:1], [2:33:2], [2:33:2]} | slice | bytes 65536 | tf_op jit(solution)/shard_map/slice | solution.py:55
  148.7 4.9 %slice.264 = bf16[1,1,64,16,16]{2,3,4,1,0:T(8,128)(2,1)} slice(bf16[3,1,64,34,34]{2,3,4,1,0:T(8,128)(2,1)S(1)} %pad.9), slice={[2:3:1], [0:1:1], [0:64:1], [0:31:2], [0:31:2]} | slice | bytes 65536 | tf_op jit(solution)/shard_map/slice | solution.py:55
  153.5 4.9 %slice.265 = bf16[1,1,64,16,16]{2,3,4,1,0:T(8,128)(2,1)} slice(bf16[3,1,64,34,34]{2,3,4,1,0:T(8,128)(2,1)S(1)} %pad.9), slice={[2:3:1], [0:1:1], [0:64:1], [0:31:2], [1:32:2]} | slice | bytes 65536 | tf_op jit(solution)/shard_map/slice | solution.py:55
  158.4 4.9 %slice.266 = bf16[1,1,64,16,16]{2,3,4,1,0:T(8,128)(2,1)} slice(bf16[3,1,64,34,34]{2,3,4,1,0:T(8,128)(2,1)S(1)} %pad.9), slice={[2:3:1], [0:1:1], [0:64:1], [0:31:2], [2:33:2]} | slice | bytes 65536 | tf_op jit(solution)/shard_map/slice | solution.py:55
  163.3 4.9 %slice.267 = bf16[1,1,64,16,16]{2,3,4,1,0:T(8,128)(2,1)} slice(bf16[3,1,64,34,34]{2,3,4,1,0:T(8,128)(2,1)S(1)} %pad.9), slice={[2:3:1], [0:1:1], [0:64:1], [1:32:2], [0:31:2]} | slice | bytes 65536 | tf_op jit(solution)/shard_map/slice | solution.py:55
  168.1 4.9 %slice.268 = bf16[1,1,64,16,16]{2,3,4,1,0:T(8,128)(2,1)} slice(bf16[3,1,64,34,34]{2,3,4,1,0:T(8,128)(2,1)S(1)} %pad.9), slice={[2:3:1], [0:1:1], [0:64:1], [1:32:2], [1:32:2]} | slice | bytes 65536 | tf_op jit(solution)/shard_map/slice | solution.py:55
  173.0 4.9 %slice.269 = bf16[1,1,64,16,16]{2,3,4,1,0:T(8,128)(2,1)} slice(bf16[3,1,64,34,34]{2,3,4,1,0:T(8,128)(2,1)S(1)} %pad.9), slice={[2:3:1], [0:1:1], [0:64:1], [1:32:2], [2:33:2]} | slice | bytes 65536 | tf_op jit(solution)/shard_map/slice | solution.py:55
  177.9 4.9 %slice.270 = bf16[1,1,64,16,16]{2,3,4,1,0:T(8,128)(2,1)} slice(bf16[3,1,64,34,34]{2,3,4,1,0:T(8,128)(2,1)S(1)} %pad.9), slice={[2:3:1], [0:1:1], [0:64:1], [2:33:2], [0:31:2]} | slice | bytes 65536 | tf_op jit(solution)/shard_map/slice | solution.py:55
  183.9 0.8 copy.128
  184.8 0.6 fusion.37
  185.5 0.7 copy.200
  186.2 1.3 maximum_bitcast_fusion
  193.9 1.0 broadcast_multiply_fusion
  194.9 4.7 %fusion.31 = bf16[2,32,8,5,32]{4,2,3,1,0:T(8,128)(2,1)S(1)} fusion(bf16[3,3,3,32,64]{4,3,2,1,0:T(8,128)(2,1)S(1)} %bitcast.719, bf16[4,64,32,1,7,2]{1,4,5,2,0,3:T(8,128)(2,1)S(1)} %slice.297, bf16[4,64,32,1,8,5]{1,4,5,2,0,3:T(8,128)(2,1)S(1)} %copy.139, pred[8,5]{0,1:T(8,128)(4,1)S(1)} %copy-done.38), kind=kOutput, calls=%fused_computation.28 | convolution fusion | flops 280133632 | bytes 1159208 | tf_op jit(solution)/shard_map/conv_general_dilated | solution.py:29
  199.8 1.1 copy.141
  200.9 1.2 reshape.283
  202.1 258.4 %all-reduce.5.cloned.1.call-done = (f32[27,32,64]{2,1,0:T(8,128)}, f32[27,64,128]{2,1,0:T(8,128)}) async-done(((f32[27,32,64]{2,1,0:T(8,128)}, f32[27,64,128]{2,1,0:T(8,128)}), (f32[27,32,64]{2,1,0:T(8,128)}, f32[27,64,128]{2,1,0:T(8,128)})) %all-reduce.5.cloned.1.call-update) | async-done | bytes 1105936 | tf_op jit(solution)/shard_map/psum | solution.py:111
  460.5 1.9 copy.393
  462.4 0.9 copy.394
  (169 shorter events, 19.3 us)
Async XLA Ops:
  7.2 29.1 %copy-start = (bf16[27,64,128]{2,1,0:T(8,128)(2,1)S(1)}, bf16[27,64,128]{2,1,0:T(8,128)(2,1)}, u32[]{:S(2)}) copy-start(bf16[27,64,128]{2,1,0:T(8,128)(2,1)} %param.7) | copy-start | bytes 1327108
  7.2 12.6 %copy-start.4 = (bf16[2,1,32,1024]{3,2,1,0:T(8,128)(2,1)S(1)}, bf16[2,1,32,1024]{3,2,1,0:T(8,128)(2,1)}, u32[]{:S(2)}) copy-start(bf16[2,1,32,1024]{3,2,1,0:T(8,128)(2,1)} %param.4) | copy-start | bytes 393220
  7.2 10.5 %copy-start.10 = (bf16[1,1,128,256]{3,2,1,0:T(8,128)(2,1)S(1)}, bf16[1,1,128,256]{3,2,1,0:T(8,128)(2,1)}, u32[]{:S(2)}) copy-start(bf16[1,1,128,256]{3,2,1,0:T(8,128)(2,1)} %param.5) | copy-start | bytes 196612
  7.2 453.3 %all-reduce.5.cloned.1.call-start = ((), (), s32[]{:S(2)}) async-start(), calls=%async_computation | async-start | bytes 2654208 | tf_op jit(solution)/shard_map/psum | solution.py:111
  8.8 14.1 %collective-permute-start.1 = (bf16[1,1,32,32,32]{3,2,0,4,1:T(8,128)(2,1)S(1)}, bf16[1,1,32,32,32]{3,2,0,4,1:T(8,128)(2,1)S(1)}, u32[]{:S(2)}, u32[]{:S(2)}) collective-permute-start(bf16[1,1,32,32,32]{3,2,0,4,1:T(8,128)(2,1)S(1)} %copy.119), channel_id=1, source_target_pairs={{1,0},{2,1},{3,2},{4,3},{5,4},{6,5},{7,6},{8,7},{9,8},{10,9},{11,1... | collective-permute-start | bytes 196616 | tf_op jit(solution)/shard_map/ppermute | solution.py:17
  14.6 8.3 %collective-permute-start = (bf16[1,1,32,32,32]{3,2,0,4,1:T(8,128)(2,1)S(1)}, bf16[1,1,32,32,32]{3,2,0,4,1:T(8,128)(2,1)S(1)}, u32[]{:S(2)}, u32[]{:S(2)}) collective-permute-start(bf16[1,1,32,32,32]{3,2,0,4,1:T(8,128)(2,1)S(1)} %copy.118), channel_id=1, source_target_pairs={{0,1},{1,2},{2,3},{3,4},{4,5},{5,6},{6,7},{7,8},{8,9},{9,10},{10,1... | collective-permute-start | bytes 196616 | tf_op jit(solution)/shard_map/ppermute | solution.py:14
  17.8 18.3 %collective-permute-start.3 = (bf16[1,1,128,16,16]{2,4,3,1,0:T(8,128)(2,1)S(1)}, bf16[1,1,128,16,16]{2,4,3,1,0:T(8,128)(2,1)S(1)}, u32[]{:S(2)}, u32[]{:S(2)}) collective-permute-start(bf16[1,1,128,16,16]{2,4,3,1,0:T(8,128)(2,1)S(1)} %bitcast.688), channel_id=1, source_target_pairs={{1,0},{2,1},{3,2},{4,3},{5,4},{6,5},{7,6},{8,7},{9,8},{10,9},{11,1... | collective-permute-start | bytes 196616 | tf_op jit(solution)/shard_map/ppermute | solution.py:25
  21.3 1.9 copy-start.2
  22.9 0.7 copy-start.6
  23.0 0.8 copy-start.8
  24.1 2.9 copy-start.36
  24.1 2.9 copy-start.38
  31.0 29.0 %collective-permute-start.2 = (bf16[1,1,64,32,32]{2,3,4,1,0:T(8,128)(2,1)S(1)}, bf16[1,1,64,32,32]{2,3,4,1,0:T(8,128)(2,1)S(1)}, u32[]{:S(2)}, u32[]{:S(2)}) collective-permute-start(bf16[1,1,64,32,32]{2,3,4,1,0:T(8,128)(2,1)S(1)} %slice_bitcast_fusion.2), channel_id=1, source_target_pairs={{0,1},{1,2},{2,3},{3,4},{4,5},{5,6},{6,7},{7,8},{8,9},{9,10},{10,1... | collective-permute-start | bytes 393224 | tf_op jit(solution)/shard_map/ppermute | solution.py:25
  36.1 0.7 copy-start.39
  38.5 147.7 %collective-permute-start.5 = (bf16[1,1,64,32,32]{2,3,4,0,1:T(8,128)(2,1)S(1)}, bf16[1,1,64,32,32]{2,3,4,0,1:T(8,128)(2,1)}, u32[]{:S(2)}, u32[]{:S(2)}) collective-permute-start(bf16[1,1,64,32,32]{2,3,4,0,1:T(8,128)(2,1)S(1)} %get-tuple-element.22), channel_id=1, source_target_pairs={{1,0},{2,1},{3,2},{4,3},{5,4},{6,5},{7,6},{8,7},{9,8},{10,9},{11,1... | collective-permute-start | bytes 393224 | tf_op jit(solution)/shard_map/ppermute | solution.py:17
  40.5 145.8 %collective-permute-start.4 = (bf16[1,1,64,32,32]{2,3,4,0,1:T(8,128)(2,1)S(1)}, bf16[1,1,64,32,32]{2,3,4,0,1:T(8,128)(2,1)}, u32[]{:S(2)}, u32[]{:S(2)}) collective-permute-start(bf16[1,1,64,32,32]{2,3,4,0,1:T(8,128)(2,1)S(1)} %get-tuple-element.21), channel_id=1, source_target_pairs={{0,1},{1,2},{2,3},{3,4},{4,5},{5,6},{6,7},{7,8},{8,9},{9,10},{10,1... | collective-permute-start | bytes 393224 | tf_op jit(solution)/shard_map/ppermute | solution.py:14
  46.3 1.0 copy-start.3
  46.3 1.1 copy-start.9
  51.1 1.0 copy-start.1
  55.7 1.0 copy-start.7
  183.9 0.9 copy-start.40
  187.8 0.8 copy-start.35
  187.8 1.0 copy-start.34
  188.3 0.9 copy-start.33
  188.3 1.0 copy-start.32
  188.3 1.2 copy-start.31
  188.3 1.4 copy-start.30
  188.3 1.6 copy-start.29
  188.4 1.8 copy-start.28
  188.4 1.9 copy-start.27
  188.5 2.0 copy-start.26
  188.5 2.2 copy-start.25
  188.5 2.4 copy-start.24
  188.8 2.3 copy-start.23
  189.2 2.1 copy-start.22
  189.4 2.1 copy-start.21
  189.5 2.1 copy-start.20
  189.7 2.1 copy-start.19
  189.9 2.1 copy-start.18
  190.1 2.1 copy-start.17
  190.3 2.1 copy-start.16
  190.5 2.1 copy-start.15
  190.7 2.1 copy-start.14
  190.9 2.1 copy-start.13
  191.1 2.0 copy-start.12
  191.3 2.0 copy-start.11
  193.9 1.0 copy-start.37
  460.5 1.9 copy-start.5
Sparse Core Ops, SparseCore 0:
  195.0 265.4 all-reduce.4
where the time goes:
time: 471 us; the launch traced here: 470 us
  waiting for transfers between devices  258 us (55%)
  local copies, waits for them, and re-layouts  143 us (30%)
  matrix products  28.3 us (6%)
  starting transfers between devices  21.4 us (5%)
  between operations  15.2 us (3%)
    psum x1, waiting for transfers between devices, local(): first_grads = lax.psum(first_grads, ('sample', 'space'))  258 us
    slice x27, local copies, waits for them, and re-layouts, weight_grad(): lax.slice(padded, (depth_tap, 0, 0, row_tap, col_tap), (depth_tap + strid...  123 us
    dot_general x54, matrix products, weight_grad(): jnp.einsum('zbiyx,zboyx->io', window, grads, preferred_element_type=jnp.f...  18.3 us
    conv_general_dilated x4, matrix products, convolve(): lax.conv_general_dilated(inputs, kernel, (stride, stride, stride), margin...  9.99 us
  transfers between devices with their start and end apart: 7, of which 1 were waited for; matrix products, arithmetic and copies ran while one was open for 34% of the time, Pallas kernels for 0%

commit v1 on v0

--- a/solution.py
+++ b/solution.py
@@ -108,7 +108,7 @@
     ).astype(jnp.bfloat16)
     padded_input = jnp.pad(framed, ((0, 0), (0, 0), (0, 0), (1, 1), (1, 1)))
     first_grads = weight_grad(padded_input, pre_grads, 1) * scale_one
-    first_grads = lax.psum(first_grads, ("sample", "space"))
+    first_grads = jnp.sum(lax.all_gather(first_grads, ("sample", "space")), axis=0)
     return (
         layer_out,
         input_grads.reshape(depth, batch, channels_in, plane),

time: 471 us -> 947 us (2.01)
  waiting for transfers between devices: 258 us -> 699 us
  other arithmetic: 3.85 us -> 39.3 us
    all_gather x0 -> x1, waiting for transfers between devices: none -> 475 us  [local(): lax.all_gather(first_grads, ('sample', 'space'))]
    reduce_sum x0 -> x1, other arithmetic: none -> 35.4 us  [local(): jnp.sum(lax.all_gather(first_grads, ('sample', 'space')), axis=0)]
    psum x1, waiting for transfers between devices: 258 us -> 224 us  [local(): second_grads = lax.psum(local_two, ('sample', 'space'))]
  transfers between devices with their start and end apart: 7 -> 8, of which waited for: 1 -> 2; matrix products, arithmetic and copies ran while one was open for 34% -> 20% of each run, Pallas kernels for 0% -> 0%
where the time goes in v1:
time: 947 us; the launch traced here: 946 us
  waiting for transfers between devices  699 us (74%)
  local copies, waits for them, and re-layouts  143 us (15%)
  other arithmetic  39.3 us (4%)
  matrix products  28.5 us (3%)
  starting transfers between devices  21.2 us (2%)
  between operations  15.3 us (2%)
    all_gather x1, waiting for transfers between devices, local(): lax.all_gather(first_grads, ('sample', 'space'))  475 us
    psum x1, waiting for transfers between devices, local(): second_grads = lax.psum(local_two, ('sample', 'space'))  224 us
    slice x27, local copies, waits for them, and re-layouts, weight_grad(): lax.slice(padded, (depth_tap, 0, 0, row_tap, col_tap), (depth_tap + strid...  123 us
    reduce_sum x1, other arithmetic, local(): jnp.sum(lax.all_gather(first_grads, ('sample', 'space')), axis=0)  35.4 us
  transfers between devices with their start and end apart: 8, of which 2 were waited for; matrix products, arithmetic and copies ran while one was open for 20% of the time, Pallas kernels for 0%

profile of v1, /device:TPU:1, one launch (start us, length us, event | category | flops | bytes accessed | tf_op | source)
XLA Modules:
  0.0 946.0 jit_solution(15627307449861322594)
XLA Ops:
  7.2 0.9 fusion.282
  8.8 5.1 collective-permute-start.1
  14.6 3.1 collective-permute-start
  17.8 1.9 collective-permute-start.3
  20.5 0.9 copy.204
  21.4 1.6 copy.241
  24.1 1.6 copy.207
  25.7 1.2 slice.285
  26.9 3.8 add_divide_fusion
  31.9 0.8 fusion.24
  34.2 0.6 fusion.92
  34.8 0.6 fusion.91
  36.7 0.6 fusion.87
  37.8 0.6 fusion.85
  38.4 0.6 fusion.84
  39.5 0.6 fusion.82
  41.4 0.6 fusion.79
  42.5 0.6 fusion.77
  43.6 0.8 fusion.75
  44.4 0.6 fusion.74
  46.2 0.6 fusion.70
  47.3 0.6 fusion.68
  47.9 0.8 broadcast_multiply_fusion.1
  49.0 4.5 collective-permute-start.2
  53.6 0.7 fusion.281
  54.3 1.9 collective-permute-start.5
  56.2 4.5 collective-permute-start.4
  61.3 4.9 slice.246
  66.3 4.9 slice.247
  71.1 4.9 slice.248
  76.0 4.9 slice.249
  80.9 4.9 slice.250
  85.8 4.9 slice.251
  90.6 4.9 slice.252
  95.5 4.9 slice.253
  100.4 4.9 slice.254
  105.3 4.9 slice.255
  110.2 4.9 slice.256
  115.0 4.9 slice.257
  119.9 4.9 slice.258
  124.8 4.9 slice.259
  129.7 4.9 slice.260
  134.6 4.9 slice.261
  139.4 4.9 slice.262
  144.3 4.9 slice.263
  149.2 4.9 slice.264
  154.1 4.9 slice.265
  158.9 4.9 slice.266
  163.8 4.9 slice.267
  168.7 4.9 slice.268
  173.6 4.9 slice.269
  178.4 4.9 slice.270
  184.4 0.8 copy.212
  185.3 0.6 fusion.37
  186.0 1.3 maximum_bitcast_fusion
  193.7 1.0 broadcast_multiply_fusion
  194.7 4.7 fusion.31
  199.5 0.7 copy.284
  200.4 1.1 copy.225
  201.5 1.2 reshape.664
  202.7 474.6 %all-gather.2.cloned.1.call-done = f32[256,27,32,64]{3,2,1,0:T(8,128)} async-done(((f32[1,27,32,64]{3,2,1,0:T(8,128)}), f32[256,27,32,64]{3,2,1,0:T(8,128)}) %all-gather.2.cloned.1.call-update) | async-done | bytes 56623120 | tf_op jit(solution)/shard_map/all_gather | solution.py:111
  677.3 35.4 %reduce_sum.9 = f32[27,32,64]{2,1,0:T(8,128)} reduce(f32[256,27,32,64]{3,2,1,0:T(8,128)} %all-gather.2.cloned.1.call-done, f32[]{:T(128)} %constant.4.clone.1), dimensions={0}, to_apply=%region_0.1 | reduce | flops 14100480 | bytes 56844292 | tf_op jit(solution)/shard_map/reduce_sum | solution.py:111
  712.7 224.3 %all-reduce.4.cloned.1.call-done = f32[27,64,128]{2,1,0:T(8,128)} async-done(((f32[27,64,128]{2,1,0:T(8,128)}), f32[27,64,128]{2,1,0:T(8,128)}) %all-reduce.4.cloned.1.call-update) | async-done | bytes 884752 | tf_op jit(solution)/shard_map/psum | solution.py:99
  937.0 2.2 copy.476
  (170 shorter events, 20.4 us)
Async XLA Ops:
  7.2 24.3 %copy-start = (bf16[27,64,128]{2,1,0:T(8,128)(2,1)S(1)}, bf16[27,64,128]{2,1,0:T(8,128)(2,1)}, u32[]{:S(2)}) copy-start(bf16[27,64,128]{2,1,0:T(8,128)(2,1)} %param.7) | copy-start | bytes 1327108
  7.2 12.6 %copy-start.4 = (bf16[2,1,32,1024]{3,2,1,0:T(8,128)(2,1)S(1)}, bf16[2,1,32,1024]{3,2,1,0:T(8,128)(2,1)}, u32[]{:S(2)}) copy-start(bf16[2,1,32,1024]{3,2,1,0:T(8,128)(2,1)} %param.4) | copy-start | bytes 393220
  7.2 10.5 %copy-start.9 = (bf16[1,1,128,256]{3,2,1,0:T(8,128)(2,1)S(1)}, bf16[1,1,128,256]{3,2,1,0:T(8,128)(2,1)}, u32[]{:S(2)}) copy-start(bf16[1,1,128,256]{3,2,1,0:T(8,128)(2,1)} %param.5) | copy-start | bytes 196612
  7.2 670.1 %all-gather.2.cloned.1.call-start = ((), (), s32[]{:S(2)}) async-start(), calls=%async_computation | async-start | bytes 113688576 | tf_op jit(solution)/shard_map/all_gather | solution.py:111
  8.8 14.1 %collective-permute-start.1 = (bf16[1,1,32,32,32]{3,2,0,4,1:T(8,128)(2,1)S(1)}, bf16[1,1,32,32,32]{3,2,0,4,1:T(8,128)(2,1)S(1)}, u32[]{:S(2)}, u32[]{:S(2)}) collective-permute-start(bf16[1,1,32,32,32]{3,2,0,4,1:T(8,128)(2,1)S(1)} %copy.203), channel_id=1, source_target_pairs={{1,0},{2,1},{3,2},{4,3},{5,4},{6,5},{7,6},{8,7},{9,8},{10,9},{11,1... | collective-permute-start | bytes 196616 | tf_op jit(solution)/shard_map/ppermute | solution.py:17
  14.6 8.3 collective-permute-start
  17.8 13.5 %collective-permute-start.3 = (bf16[1,1,128,16,16]{2,4,3,1,0:T(8,128)(2,1)S(1)}, bf16[1,1,128,16,16]{2,4,3,1,0:T(8,128)(2,1)S(1)}, u32[]{:S(2)}, u32[]{:S(2)}) collective-permute-start(bf16[1,1,128,16,16]{2,4,3,1,0:T(8,128)(2,1)S(1)} %bitcast.688), channel_id=1, source_target_pairs={{1,0},{2,1},{3,2},{4,3},{5,4},{6,5},{7,6},{8,7},{9,8},{10,9},{11,1... | collective-permute-start | bytes 196616 | tf_op jit(solution)/shard_map/ppermute | solution.py:25
  21.3 1.9 copy-start.2
  22.9 0.7 copy-start.5
  22.9 0.8 copy-start.7
  24.1 2.8 copy-start.35
  24.1 2.8 copy-start.37
  31.3 0.7 copy-start.38
  34.7 1.0 copy-start.3
  34.8 1.1 copy-start.8
  39.5 1.0 copy-start.1
  44.4 1.0 copy-start.6
  48.7 888.2 %all-reduce.4.cloned.1.call-start = ((), (), s32[]{:S(2)}) async-start(), calls=%async_computation.1 | async-start | bytes 1769472 | tf_op jit(solution)/shard_map/psum | solution.py:99
  49.0 11.8 %collective-permute-start.2 = (bf16[1,1,64,32,32]{2,3,4,1,0:T(8,128)(2,1)S(1)}, bf16[1,1,64,32,32]{2,3,4,1,0:T(8,128)(2,1)S(1)}, u32[]{:S(2)}, u32[]{:S(2)}) collective-permute-start(bf16[1,1,64,32,32]{2,3,4,1,0:T(8,128)(2,1)S(1)} %slice_bitcast_fusion.2), channel_id=1, source_target_pairs={{0,1},{1,2},{2,3},{3,4},{4,5},{5,6},{6,7},{7,8},{8,9},{9,10},{10,1... | collective-permute-start | bytes 393224 | tf_op jit(solution)/shard_map/ppermute | solution.py:25
  54.3 131.6 %collective-permute-start.5 = (bf16[1,1,64,32,32]{2,3,4,0,1:T(8,128)(2,1)}, bf16[1,1,64,32,32]{2,3,4,0,1:T(8,128)(2,1)}, u32[]{:S(2)}, u32[]{:S(2)}) collective-permute-start(bf16[1,1,64,32,32]{2,3,4,0,1:T(8,128)(2,1)} %get-tuple-element.24), channel_id=1, source_target_pairs={{1,0},{2,1},{3,2},{4,3},{5,4},{6,5},{7,6},{8,7},{9,8},{10,9},{11,1... | collective-permute-start | bytes 393224 | tf_op jit(solution)/shard_map/ppermute | solution.py:17
  56.2 129.7 %collective-permute-start.4 = (bf16[1,1,64,32,32]{2,3,4,0,1:T(8,128)(2,1)S(1)}, bf16[1,1,64,32,32]{2,3,4,0,1:T(8,128)(2,1)}, u32[]{:S(2)}, u32[]{:S(2)}) collective-permute-start(bf16[1,1,64,32,32]{2,3,4,0,1:T(8,128)(2,1)S(1)} %get-tuple-element.23), channel_id=1, source_target_pairs={{0,1},{1,2},{2,3},{3,4},{4,5},{5,6},{6,7},{7,8},{8,9},{9,10},{10,1... | collective-permute-start | bytes 393224 | tf_op jit(solution)/shard_map/ppermute | solution.py:14
  184.4 0.9 copy-start.39
  187.6 0.8 copy-start.34
  187.6 1.0 copy-start.33
  188.1 0.9 copy-start.32
  188.1 1.0 copy-start.31
  188.1 1.2 copy-start.30
  188.1 1.4 copy-start.29
  188.1 1.6 copy-start.28
  188.2 1.8 copy-start.27
  188.2 1.9 copy-start.26
  188.3 2.0 copy-start.25
  188.3 2.2 copy-start.24
  188.3 2.4 copy-start.23
  188.6 2.3 copy-start.22
  189.0 2.1 copy-start.21
  189.1 2.1 copy-start.20
  189.3 2.1 copy-start.19
  189.5 2.1 copy-start.18
  189.7 2.1 copy-start.17
  189.9 2.1 copy-start.16
  190.1 2.1 copy-start.15
  190.3 2.1 copy-start.14
  190.5 2.1 copy-start.13
  190.7 2.1 copy-start.12
  190.9 2.0 copy-start.11
  191.1 2.0 copy-start.10
  193.2 1.6 copy-start.36
Sparse Core Ops, SparseCore 0:
  48.9 628.3 all-gather.1
  683.3 253.6 all-reduce.3
